TPU v7x, 32 devices: a whole 2x2x4 slice. The times are simulated.
32 devices in a mesh: groups: 2 (over y), lat: 16 (over z, x, core).
Axes of the slice: x: 2, y: 2, z: 4, core: 2. Of those that a mesh axis runs over, the one named last changes fastest.
Arguments:
- latent: bfloat16 [16384, 1536], P(('groups', 'lat')), parts along dimension 0, may hold values from -400 to 400
- query_gain: float32 [1536], replicated, may hold values from 0.1 to 1.9
- key_gain: float32 [1536], replicated, may hold values from 0.1 to 1.9
- output_gain: float32 [1536], replicated, may hold values from 0.1 to 1.9
- output_weight: bfloat16 [1536, 1536], replicated, may hold values from -0.15625 to 0.15625
- observations: bfloat16 [128, 128, 128], P(('groups', 'lat')), parts along dimension 0, may hold values from -6 to 6
- panels: bfloat16 [1024, 1536], P('lat'), may hold values from -0.5 to 0.5
- instrument: int32 [128], P('groups'), parts along dimension 0, may hold values from 0 to 7
- observed_count: int32 [128], P('groups'), parts along dimension 0, may hold values from 1 to 128
- footprint: int32 [128, 6], P(('groups', 'lat')), parts along dimension 0, may hold values from 0 to 63, as said below
- tile_blocks: int32 [128], P(('groups', 'lat')), parts along dimension 0, may hold values from 1 to 6
Outputs:
- encoded: bfloat16 [16384, 1536], P(('groups', 'lat')), parts along dimension 0
There are 2 independent parts, one for each index of `groups`. A program takes and returns all parts, laid end to end along the dimension named above; an argument that names none is the same for every part. Nothing has to cross between parts.
Inputs may be any that keep to these rules, and one draw needn't show every extreme that they name: `footprint`: tile t lies on latitude device t // 4 and block b on b // 4; every entry of tile t's list names a block on that device or on one of the two beside it.
All inputs are finite; a program needn't handle non-finite values.
Results may differ from a plain program's by a relative error of at most 0.0039.
Values may be sent and summed in bfloat16 or wider, within the bound.
No kernel may reach another device: no remote copies, remote signals or barrier semaphores. Data moves between devices by JAX's collectives and lax.ppermute only.
A program may use at most 128 MiB of HBM per device.

v0:
```python
import math
import jax
import jax.numpy as jnp
from jax import lax
from jax.sharding import PartitionSpec as P

D = 1536
HD = 64
NINST = 8
CH = 128
CELLS = 128
OBS = 128
MAXB = 6


def padded(value, sides, width):
    for axis, dim in sides:
        peers, length = (lax.axis_size(axis), value.shape[dim])
        up = [(i, (i + 1) % peers) for i in range(peers - 1)]
        down = [(j, i) for i, j in up]
        last = lax.slice_in_dim(value, length - width, length, axis=dim)
        first = lax.slice_in_dim(value, 0, width, axis=dim)
        before = lax.ppermute(last, axis, up)
        after = lax.ppermute(first, axis, down)
        value = jnp.concatenate([before, value, after], axis=dim)
    return value


def normalize(values, gain):
    values = values.astype(jnp.float32)
    return values * lax.rsqrt(jnp.mean(values * values, axis=-1, keepdims=True) + 1e-06) * gain


def body(
    latent,
    query_gain,
    key_gain,
    output_gain,
    output_weight,
    observations,
    panels,
    instrument,
    observed_count,
    footprint,
    tile_blocks,
):
    block_count = observations.shape[0]
    position = lax.axis_index("lat")
    first_block = (position - 1) * block_count
    all_blocks = instrument.shape[0]
    table = lax.all_gather(panels, "lat", axis=0, tiled=True)
    near_count = 3 * block_count
    near_ids = jnp.clip(first_block + jnp.arange(near_count, dtype=jnp.int32), 0, all_blocks - 1)
    kind_range = jnp.arange(NINST, dtype=jnp.int32)
    own_kinds = lax.dynamic_slice_in_dim(instrument, position * block_count, block_count)
    select = (own_kinds[:, None] == kind_range[None, :]).astype(jnp.bfloat16)
    widened = (observations[:, :, None, :] * select[:, None, :, None]).reshape(
        observations.shape[0], OBS, NINST * CH
    )
    embedded = jnp.einsum("bop,pd->bod", widened, table, preferred_element_type=jnp.float32).astype(
        jnp.bfloat16
    )
    nearby = padded(embedded, (("lat", 0),), block_count)
    keys = normalize(nearby, key_gain).astype(jnp.bfloat16)
    counts = observed_count[near_ids]
    tiles = latent.shape[0] // CELLS
    heads = D // HD
    keys_t = keys.reshape(near_count, OBS, heads, HD).transpose(0, 2, 3, 1)
    values_t = nearby.reshape(near_count, OBS, heads, HD).transpose(0, 2, 3, 1)
    queries = (latent.astype(jnp.float32) * query_gain).astype(jnp.bfloat16)
    queries_t = queries.reshape(tiles, CELLS, heads, HD).transpose(0, 2, 3, 1)
    local_ids = footprint - first_block
    scale = 1.0 / math.sqrt(HD)
    slot_rows = jnp.arange(OBS, dtype=jnp.int32)
    near_range = jnp.arange(near_count, dtype=jnp.int32)

    def attend(slot_index, carry):
        running, total, accum = carry
        chosen = lax.dynamic_index_in_dim(local_ids, slot_index, 1, keepdims=False)
        pick = chosen[:, None] == near_range[None, :]
        select = pick.astype(jnp.bfloat16)
        slot_keys = jnp.einsum(
            "tn,nhdk->thdk", select, keys_t, preferred_element_type=jnp.float32
        ).astype(jnp.bfloat16)
        slot_values = jnp.einsum(
            "tn,nhdk->thdk", select, values_t, preferred_element_type=jnp.float32
        ).astype(jnp.bfloat16)
        slot_counts = jnp.sum(jnp.where(pick, counts[None, :], 0), axis=1)
        scores = (
            jnp.einsum("thdq,thdk->thqk", queries_t, slot_keys, preferred_element_type=jnp.float32)
            * scale
        )
        usable = (slot_index < tile_blocks)[:, None] & (slot_rows[None, :] < slot_counts[:, None])
        usable = usable[:, None, None, :]
        highest = jnp.maximum(running, jnp.max(jnp.where(usable, scores, -1e30), axis=-1))
        factor = jnp.exp(running - highest)
        weights = jnp.where(usable, jnp.exp(scores - highest[..., None]), 0.0)
        total = total * factor + jnp.sum(weights, axis=-1)
        update = jnp.einsum(
            "thdk,thqk->thdq",
            slot_values,
            weights.astype(jnp.bfloat16),
            preferred_element_type=jnp.float32,
        )
        accum = accum * factor[:, :, None, :] + update
        return (highest, total, accum)

    start = (
        jnp.full((tiles, heads, CELLS), -1e30, jnp.float32),
        jnp.zeros((tiles, heads, CELLS), jnp.float32),
        jnp.zeros((tiles, heads, HD, CELLS), jnp.float32),
    )
    running, total, accum = lax.fori_loop(0, MAXB, attend, start)
    attended = (
        (accum / total[:, :, None, :])
        .astype(jnp.bfloat16)
        .transpose(0, 3, 1, 2)
        .reshape(tiles * CELLS, D)
    )
    mixed = latent.astype(jnp.float32) + jnp.dot(
        attended, output_weight, preferred_element_type=jnp.float32
    )
    return normalize(mixed, output_gain).astype(jnp.bfloat16)


def solution(mesh):
    return jax.shard_map(
        body,
        mesh=mesh,
        in_specs=(
            P(("groups", "lat"), None),
            P(),
            P(),
            P(),
            P(),
            P(("groups", "lat"), None, None),
            P("lat", None),
            P("groups"),
            P("groups"),
            P(("groups", "lat"), None),
            P(("groups", "lat")),
        ),
        out_specs=P(("groups", "lat"), None),
        check_vma=False,
    )
```

profile of v0, /device:TPU:1, one launch (start us, length us, event | category | flops | bytes accessed | tf_op | source)
XLA Modules:
  0.0 224.9 jit_solution(17268411297548896115)
XLA Ops:
  6.5 0.7 all-gather.2.cloned.1.call-update
  7.3 0.7 dynamic_slice.11
  8.2 1.0 mul.112
  9.7 47.9 %all-gather.2.cloned.1.call-done = bf16[1024,1536]{1,0:T(8,128)(2,1)} async-done(((bf16[64,1536]{1,0:T(8,128)(2,1)}), bf16[1024,1536]{1,0:T(8,128)(2,1)}) %all-gather.2.cloned.1.call-update) | async-done | bytes 3145744 | tf_op jit(solution)/shard_map/all_gather | solution.py:51
  57.6 5.0 %fusion.30 = bf16[4,128,1536]{2,1,0:T(8,128)(2,1)} fusion(bf16[1024,1536]{1,0:T(8,128)(2,1)} %all-gather.2.cloned.1.call-done, bf16[4,128,1024]{2,1,0:T(8,128)(2,1)S(1)} %mul.113, bf16[4,1024]{1,0:T(4,128)(2,1)S(1)} %bitcast.76), kind=kOutput, calls=%fused_computation.47 | convolution fusion | flops 1611923456 | bytes 5775360 | tf_op jit(solution)/shard_map/bop,pd->bod/dot_general | solution.py:60
  62.5 2.2 collective-permute-start.1
  64.7 3.4 %collective-permute-start = (bf16[4,128,1536]{2,1,0:T(8,128)(2,1)}, bf16[4,128,1536]{2,1,0:T(8,128)(2,1)}, u32[]{:S(2)}, u32[]{:S(2)}) collective-permute-start(bf16[4,128,1536]{2,1,0:T(8,128)(2,1)} %fusion.30), channel_id=1, source_target_pairs={{0,1},{1,2},{2,3},{3,4},{4,5},{5,6},{6,7},{7,8},{8,9},{9,10},{10,1... | collective-permute-start | bytes 4718600 | tf_op jit(solution)/shard_map/ppermute | solution.py:23
  68.6 0.7 copy.35
  70.2 0.7 gather_fusion
  70.9 1.9 copy.33
  72.8 11.8 %collective-permute-done.1 = bf16[4,128,1536]{2,1,0:T(8,128)(2,1)} collective-permute-done((bf16[4,128,1536]{2,1,0:T(8,128)(2,1)}, bf16[4,128,1536]{2,1,0:T(8,128)(2,1)}, u32[]{:S(2)}, u32[]{:S(2)}) %collective-permute-start.1) | collective-permute-done | bytes 1572896 | tf_op jit(solution)/shard_map/ppermute | solution.py:24
  84.6 16.1 %collective-permute-done = bf16[4,128,1536]{2,1,0:T(8,128)(2,1)} collective-permute-done((bf16[4,128,1536]{2,1,0:T(8,128)(2,1)}, bf16[4,128,1536]{2,1,0:T(8,128)(2,1)}, u32[]{:S(2)}, u32[]{:S(2)}) %collective-permute-start) | collective-permute-done | bytes 1572896 | tf_op jit(solution)/shard_map/ppermute | solution.py:23
  100.7 5.7 %multiply_reduce_fusion = (f32[12,128]{1,0:T(8,128)S(1)}, bf16[12,128,1536]{2,1,0:T(8,128)(2,1)}) fusion(bf16[4,128,1536]{2,1,0:T(8,128)(2,1)} %collective-permute-done.1, bf16[4,128,1536]{2,1,0:T(8,128)(2,1)} %fusion.30, bf16[4,128,1536]{2,1,0:T(8,128)(2,1)} %collective-permute-done), kind=kLoop, calls=%fused_computation.36 | loop fusion | flops 11794944 | bytes 9443328 | tf_op jit(solution)/shard_map/reduce_sum | solution.py:31
  106.4 2.6 %copy.34 = bf16[4,128,1536]{1,2,0:T(8,128)(2,1)} copy(bf16[4,128,1536]{2,1,0:T(8,128)(2,1)} %collective-permute-done.1) | data formatting | bytes 3145728 | tf_op jit(solution)/shard_map/ppermute | solution.py:24
  109.0 2.6 %copy.32 = bf16[4,128,1536]{1,2,0:T(8,128)(2,1)} copy(bf16[4,128,1536]{2,1,0:T(8,128)(2,1)} %collective-permute-done) | data formatting | bytes 3145728 | tf_op jit(solution)/shard_map/ppermute | solution.py:23
  111.6 3.7 %fusion.26 = bf16[12,24,64,128]{3,2,1,0:T(8,128)(2,1)S(1)} fusion(bf16[4,128,24,64]{1,3,2,0:T(8,128)(2,1)} %bitcast.73, bf16[4,128,24,64]{1,3,2,0:T(8,128)(2,1)S(1)} %bitcast.72, bf16[4,128,24,64]{1,3,2,0:T(8,128)(2,1)} %bitcast.74, f32[24,64]{1,0:T(8,128)S(1)} %mul.122, f32[12,128]{1,0:T(8,128)S(1)} %add_rsqrt_fusion), kind=kLoop, calls=%fused_computation.37 | loop fusion | flops 14155776 | bytes 9449472 | tf_op jit(solution)/shard_map/transpose | solution.py:68
  115.2 6.9 %copy.37 = bf16[12,24,64,128]{3,0,2,1:T(8,128)(2,1)} copy(bf16[12,24,64,128]{3,2,1,0:T(8,128)(2,1)S(1)} %fusion.26) | data formatting | bytes 9437184
  122.2 9.1 %copy.43 = bf16[12,128,1536]{1,0,2:T(8,128)(2,1)} copy(bf16[12,128,1536]{2,1,0:T(8,128)(2,1)} %get-tuple-element.287) | data formatting | bytes 9437184 | tf_op jit(solution)/shard_map/transpose | solution.py:69
  131.3 78.2 %while.18 = (s32[]{:T(128)}, f32[4,24,128]{2,1,0:T(8,128)S(1)}, f32[4,24,128]{2,1,0:T(8,128)S(1)}, f32[4,24,64,128]{3,2,1,0:T(8,128)}, s32[4]{0:T(128)S(1)}, /*i...) while((s32[]{:T(128)}, f32[4,24,128]{2,1,0:T(8,128)S(1)}, ...), condition=%wide.region_5.6_spmd.clone, body=%wide.region_1.5_spmd.clone.sunk | while | flops 461698304 | bytes 87296416 | solution.py:113
  131.6 4.0 %convolution_convert_fusion.5 = bf16[4,24,64,128]{3,0,2,1:T(4,128)(2,1)S(1)} fusion(bf16[12,24,64,128]{3,0,2,1:T(8,128)(2,1)} %get-tuple-element.394, s32[4]{0:T(128)S(1)} %dynamic-slice_bitcast_fusion.2), kind=kOutput, calls=%fused_computation.14.clone.1 | convolution fusion | flops 19660848 | bytes 6291472 | tf_op jit(solution)/shard_map/while/body/eval_jaxpr/tn,nhdk->thdk/dot_general | solution.py:85
  135.5 0.6 copy-done.2
  136.2 1.0 convolution_convert_fusion.4
  137.2 1.8 select_reduce_fusion.2
  139.0 1.7 bitcast_reduce_fusion.2
  140.9 1.8 fusion.63
  142.7 1.6 copy-done.4
  144.6 4.0 %convolution_convert_fusion.5 = bf16[4,24,64,128]{3,0,2,1:T(4,128)(2,1)S(1)} fusion(bf16[12,24,64,128]{3,0,2,1:T(8,128)(2,1)} %get-tuple-element.394, s32[4]{0:T(128)S(1)} %dynamic-slice_bitcast_fusion.2), kind=kOutput, calls=%fused_computation.14.clone.1 | convolution fusion | flops 19660848 | bytes 6291472 | tf_op jit(solution)/shard_map/while/body/eval_jaxpr/tn,nhdk->thdk/dot_general | solution.py:85
  148.6 0.6 copy-done.2
  149.2 1.0 convolution_convert_fusion.4
  150.2 1.8 select_reduce_fusion.2
  152.0 1.7 bitcast_reduce_fusion.2
  153.9 1.8 fusion.63
  155.7 1.6 copy-done.4
  157.6 4.0 %convolution_convert_fusion.5 = bf16[4,24,64,128]{3,0,2,1:T(4,128)(2,1)S(1)} fusion(bf16[12,24,64,128]{3,0,2,1:T(8,128)(2,1)} %get-tuple-element.394, s32[4]{0:T(128)S(1)} %dynamic-slice_bitcast_fusion.2), kind=kOutput, calls=%fused_computation.14.clone.1 | convolution fusion | flops 19660848 | bytes 6291472 | tf_op jit(solution)/shard_map/while/body/eval_jaxpr/tn,nhdk->thdk/dot_general | solution.py:85
  161.6 0.6 copy-done.2
  162.2 1.0 convolution_convert_fusion.4
  163.3 1.8 select_reduce_fusion.2
  165.1 1.7 bitcast_reduce_fusion.2
  167.0 1.8 fusion.63
  168.8 1.6 copy-done.4
  170.7 4.0 %convolution_convert_fusion.5 = bf16[4,24,64,128]{3,0,2,1:T(4,128)(2,1)S(1)} fusion(bf16[12,24,64,128]{3,0,2,1:T(8,128)(2,1)} %get-tuple-element.394, s32[4]{0:T(128)S(1)} %dynamic-slice_bitcast_fusion.2), kind=kOutput, calls=%fused_computation.14.clone.1 | convolution fusion | flops 19660848 | bytes 6291472 | tf_op jit(solution)/shard_map/while/body/eval_jaxpr/tn,nhdk->thdk/dot_general | solution.py:85
  174.6 0.6 copy-done.2
  175.3 1.0 convolution_convert_fusion.4
  176.3 1.8 select_reduce_fusion.2
  178.1 1.7 bitcast_reduce_fusion.2
  180.0 1.8 fusion.63
  181.8 1.6 copy-done.4
  183.7 4.0 %convolution_convert_fusion.5 = bf16[4,24,64,128]{3,0,2,1:T(4,128)(2,1)S(1)} fusion(bf16[12,24,64,128]{3,0,2,1:T(8,128)(2,1)} %get-tuple-element.394, s32[4]{0:T(128)S(1)} %dynamic-slice_bitcast_fusion.2), kind=kOutput, calls=%fused_computation.14.clone.1 | convolution fusion | flops 19660848 | bytes 6291472 | tf_op jit(solution)/shard_map/while/body/eval_jaxpr/tn,nhdk->thdk/dot_general | solution.py:85
  187.7 0.6 copy-done.2
  188.3 1.0 convolution_convert_fusion.4
  189.3 1.8 select_reduce_fusion.2
  191.2 1.7 bitcast_reduce_fusion.2
  193.0 1.8 fusion.63
  194.9 1.6 copy-done.4
  196.8 4.0 %convolution_convert_fusion.5 = bf16[4,24,64,128]{3,0,2,1:T(4,128)(2,1)S(1)} fusion(bf16[12,24,64,128]{3,0,2,1:T(8,128)(2,1)} %get-tuple-element.394, s32[4]{0:T(128)S(1)} %dynamic-slice_bitcast_fusion.2), kind=kOutput, calls=%fused_computation.14.clone.1 | convolution fusion | flops 19660848 | bytes 6291472 | tf_op jit(solution)/shard_map/while/body/eval_jaxpr/tn,nhdk->thdk/dot_general | solution.py:85
  201.4 1.0 convolution_convert_fusion.4
  202.4 1.8 select_reduce_fusion.2
  204.2 1.7 bitcast_reduce_fusion.2
  206.1 1.8 fusion.63
  207.9 1.6 copy-done.4
  209.5 2.5 %fusion.35 = bf16[4,128,24,64]{1,3,2,0:T(8,128)(2,1)S(1)} fusion(f32[4,24,64,128]{3,2,1,0:T(8,128)} %get-tuple-element.205, f32[4,24,128]{2,1,0:T(8,128)S(1)} %get-tuple-element.206), kind=kLoop, calls=%fused_computation.50 | loop fusion | flops 1572864 | bytes 4767744 | tf_op jit(solution)/shard_map/transpose | solution.py:117
  212.1 1.4 copy.40
  213.5 3.0 %multiply_reduce_fusion.1 = (f32[512]{0:T(512)S(1)}, f32[512,1536]{1,0:T(8,128)S(1)}) fusion(bf16[1536,1536]{1,0:T(8,128)(2,1)S(1)} %copy-done.11, bf16[192,8,4,128]{3,2,1,0:T(4,128)(2,1)S(1)} %bitcast.75, bf16[512,1536]{1,0:T(8,128)(2,1)S(1)} %copy-done.6), kind=kOutput, calls=%fused_computation.45 | convolution fusion | flops 2419064320 | bytes 11012096 | tf_op jit(solution)/shard_map/dot_general | solution.py:120
  216.6 1.5 multiply_convert_fusion.1
  (105 shorter events, 5.6 us)
Async XLA Ops:
  6.5 63.6 %copy-start = (s32[64]{0:T(128)S(1)}, s32[64]{0:T(128)}, u32[]{:S(2)}) copy-start(s32[64]{0:T(128)} %param.21) | copy-start | bytes 772
  6.5 51.0 %all-gather.2.cloned.1.call-start = ((), (), s32[]{:S(2)}) async-start(), calls=%async_computation | async-start | bytes 3342336 | tf_op jit(solution)/shard_map/all_gather | solution.py:51
  57.6 10.6 %copy-start.10 = (s32[4,6]{1,0:T(4,128)S(1)}, s32[4,6]{1,0:T(4,128)}, u32[]{:S(2)}) copy-start(s32[4,6]{1,0:T(4,128)} %param.22) | copy-start | bytes 292
  57.6 10.7 %copy-start.9 = (f32[1536]{0:T(1024)S(1)}, f32[1536]{0:T(1024)}, u32[]{:S(2)}) copy-start(f32[1536]{0:T(1024)} %param.15) | copy-start | bytes 18436
  57.6 10.7 %copy-start.5 = (bf16[512,1536]{1,0:T(8,128)(2,1)S(1)}, bf16[512,1536]{1,0:T(8,128)(2,1)}, u32[]{:S(2)}) copy-start(bf16[512,1536]{1,0:T(8,128)(2,1)} %param.13) | copy-start | bytes 4718596
  57.6 10.7 %copy-start.7 = (f32[1536]{0:T(1024)S(1)}, f32[1536]{0:T(1024)}, u32[]{:S(2)}) copy-start(f32[1536]{0:T(1024)} %param.14) | copy-start | bytes 18436
  62.5 22.0 %collective-permute-start.1 = (bf16[4,128,1536]{2,1,0:T(8,128)(2,1)}, bf16[4,128,1536]{2,1,0:T(8,128)(2,1)}, u32[]{:S(2)}, u32[]{:S(2)}) collective-permute-start(bf16[4,128,1536]{2,1,0:T(8,128)(2,1)} %fusion.30), channel_id=1, source_target_pairs={{1,0},{2,1},{3,2},{4,3},{5,4},{6,5},{7,6},{8,7},{9,8},{10,9},{11,1... | collective-permute-start | bytes 4718600 | tf_op jit(solution)/shard_map/ppermute | solution.py:24
  64.7 36.0 %collective-permute-start = (bf16[4,128,1536]{2,1,0:T(8,128)(2,1)}, bf16[4,128,1536]{2,1,0:T(8,128)(2,1)}, u32[]{:S(2)}, u32[]{:S(2)}) collective-permute-start(bf16[4,128,1536]{2,1,0:T(8,128)(2,1)} %fusion.30), channel_id=1, source_target_pairs={{0,1},{1,2},{2,3},{3,4},{4,5},{5,6},{6,7},{7,8},{8,9},{9,10},{10,1... | collective-permute-start | bytes 4718600 | tf_op jit(solution)/shard_map/ppermute | solution.py:23
  122.2 9.1 %copy-start.12 = (s32[4]{0:T(128)S(1)}, s32[4]{0:T(128)}, u32[]{:S(2)}) copy-start(s32[4]{0:T(128)} %param.23) | copy-start | bytes 52
  131.5 4.6 %copy-start.2 = (bf16[12,24,64,128]{3,0,2,1:T(8,128)(2,1)S(1)}, bf16[12,24,64,128]{3,0,2,1:T(8,128)(2,1)}, u32[]{:S(2)}) copy-start(bf16[12,24,64,128]{3,0,2,1:T(8,128)(2,1)} %get-tuple-element.392) | copy-start | bytes 14155780 | tf_op jit(solution)/shard_map/while
  139.0 1.9 copy-start.3
  142.7 1.6 copy-start.4
  144.6 4.6 %copy-start.2 = (bf16[12,24,64,128]{3,0,2,1:T(8,128)(2,1)S(1)}, bf16[12,24,64,128]{3,0,2,1:T(8,128)(2,1)}, u32[]{:S(2)}) copy-start(bf16[12,24,64,128]{3,0,2,1:T(8,128)(2,1)} %get-tuple-element.392) | copy-start | bytes 14155780 | tf_op jit(solution)/shard_map/while
  152.0 1.9 copy-start.3
  155.7 1.6 copy-start.4
  157.6 4.6 %copy-start.2 = (bf16[12,24,64,128]{3,0,2,1:T(8,128)(2,1)S(1)}, bf16[12,24,64,128]{3,0,2,1:T(8,128)(2,1)}, u32[]{:S(2)}) copy-start(bf16[12,24,64,128]{3,0,2,1:T(8,128)(2,1)} %get-tuple-element.392) | copy-start | bytes 14155780 | tf_op jit(solution)/shard_map/while
  165.1 1.9 copy-start.3
  168.8 1.6 copy-start.4
  170.7 4.6 %copy-start.2 = (bf16[12,24,64,128]{3,0,2,1:T(8,128)(2,1)S(1)}, bf16[12,24,64,128]{3,0,2,1:T(8,128)(2,1)}, u32[]{:S(2)}) copy-start(bf16[12,24,64,128]{3,0,2,1:T(8,128)(2,1)} %get-tuple-element.392) | copy-start | bytes 14155780 | tf_op jit(solution)/shard_map/while
  178.1 1.9 copy-start.3
  181.8 1.6 copy-start.4
  183.7 4.6 %copy-start.2 = (bf16[12,24,64,128]{3,0,2,1:T(8,128)(2,1)S(1)}, bf16[12,24,64,128]{3,0,2,1:T(8,128)(2,1)}, u32[]{:S(2)}) copy-start(bf16[12,24,64,128]{3,0,2,1:T(8,128)(2,1)} %get-tuple-element.392) | copy-start | bytes 14155780 | tf_op jit(solution)/shard_map/while
  191.1 1.9 copy-start.3
  194.8 1.6 copy-start.4
  196.7 4.6 %copy-start.2 = (bf16[12,24,64,128]{3,0,2,1:T(8,128)(2,1)S(1)}, bf16[12,24,64,128]{3,0,2,1:T(8,128)(2,1)}, u32[]{:S(2)}) copy-start(bf16[12,24,64,128]{3,0,2,1:T(8,128)(2,1)} %get-tuple-element.392) | copy-start | bytes 14155780 | tf_op jit(solution)/shard_map/while
  204.2 1.9 copy-start.3
  207.9 1.6 copy-start.4
  209.5 4.0 %copy-start.6 = (bf16[512,1536]{1,0:T(8,128)(2,1)S(1)}, bf16[512,1536]{1,0:T(8,128)(2,1)}, u32[]{:S(2)}) copy-start(bf16[512,1536]{1,0:T(8,128)(2,1)} %param.13) | copy-start | bytes 4718596
  209.5 4.0 %copy-start.11 = (bf16[1536,1536]{1,0:T(8,128)(2,1)S(1)}, bf16[1536,1536]{1,0:T(8,128)(2,1)}, u32[]{:S(2)}) copy-start(bf16[1536,1536]{1,0:T(8,128)(2,1)} %param.17) | copy-start | bytes 14155780
  213.5 3.0 %copy-start.8 = (f32[1536]{0:T(1024)S(1)}, f32[1536]{0:T(1024)}, u32[]{:S(2)}) copy-start(f32[1536]{0:T(1024)} %param.16) | copy-start | bytes 18436
  213.5 4.5 %copy-start.1 = (s32[64]{0:T(128)S(1)}, s32[64]{0:T(128)}, u32[]{:S(2)}) copy-start(s32[64]{0:T(128)} %param.21) | copy-start | bytes 772
Sparse Core Ops, SparseCore 0:
  9.6 47.9 all-gather.1
where the time goes:
time: 226 us; the launch traced here: 225 us
  waiting for transfers between devices  76.5 us (34%)
  matrix products  59.3 us (26%)
  local copies, waits for them, and re-layouts  43.7 us (19%)
  other arithmetic  25.7 us (11%)
  between operations  13.6 us (6%)
  starting transfers between devices  5.56 us (2%)
    all_gather x1, waiting for transfers between devices, body(): table = lax.all_gather(panels, 'lat', axis=0, tiled=True)  47.9 us
    dot_general x6, matrix products, attend(): jnp.einsum('tn,nhdk->thdk', select, values_t, preferred_element_type=jnp....  23.8 us
    ppermute x1, waiting for transfers between devices, padded(): before = lax.ppermute(last, axis, up)  16.1 us
    while x42, local copies, waits for them, and re-layouts  14.5 us
    ppermute x1, waiting for transfers between devices, padded(): after = lax.ppermute(first, axis, down)  11.8 us
    dot_general x6, matrix products, attend(): jnp.einsum('thdk,thqk->thdq', slot_values, weights.astype(jnp.bfloat16),...  10.8 us
    dot_general x6, matrix products, attend(): jnp.einsum('thdq,thdk->thqk', queries_t, slot_keys, preferred_element_typ...  10.7 us
    reduce_sum x6, other arithmetic, attend(): total = total * factor + jnp.sum(weights, axis=-1)  10 us
  transfers between devices with their start and end apart: 3, of which 3 were waited for; matrix products, arithmetic and copies ran while one was open for 3% of the time, Pallas kernels for 0%

commit v1 on v0

--- a/solution.py
+++ b/solution.py
@@ -11,6 +11,24 @@
 CELLS = 128
 OBS = 128
 MAXB = 6
+
+
+def gather_around(shard, axis, dim):
+    ways, here, step = (lax.axis_size(axis), lax.axis_index(axis), shard.shape[dim])
+    dims = [n * ways if d == dim else n for d, n in enumerate(shard.shape)]
+    full = lax.dynamic_update_slice_in_dim(
+        jnp.zeros(dims, shard.dtype), shard, here * step, axis=dim
+    )
+    going_up = going_down = shard
+    for far in range(1, ways // 2 + 1):
+        going_up = lax.ppermute(going_up, axis, [(d, (d + 1) % ways) for d in range(ways)])
+        full = lax.dynamic_update_slice_in_dim(full, going_up, (here - far) % ways * step, axis=dim)
+        if 2 * far < ways:
+            going_down = lax.ppermute(going_down, axis, [(d, (d - 1) % ways) for d in range(ways)])
+            full = lax.dynamic_update_slice_in_dim(
+                full, going_down, (here + far) % ways * step, axis=dim
+            )
+    return full
 
 
 def padded(value, sides, width):
@@ -48,7 +66,7 @@
     position = lax.axis_index("lat")
     first_block = (position - 1) * block_count
     all_blocks = instrument.shape[0]
-    table = lax.all_gather(panels, "lat", axis=0, tiled=True)
+    table = gather_around(panels, "lat", 0)
     near_count = 3 * block_count
     near_ids = jnp.clip(first_block + jnp.arange(near_count, dtype=jnp.int32), 0, all_blocks - 1)
     kind_range = jnp.arange(NINST, dtype=jnp.int32)

time: 226 us -> 213 us (0.942)
  starting transfers between devices: 5.56 us -> 47.4 us
  waiting for transfers between devices: 76.5 us -> 36.8 us
  between operations: 13.6 us -> 0.45 us
    all_gather x1 -> x0, waiting for transfers between devices: 47.9 us -> none  [body(): table = lax.all_gather(panels, 'lat', axis=0, tiled=True)]
    ppermute x0 -> x15, starting transfers between devices: none -> 36.6 us  [the longest x7 32.5 us: gather_around(): lax.ppermute(going_down, axis, [(d, (d - 1) % ways) for d in range(ways)])]
    ppermute x0 -> x15, waiting for transfers between devices: none -> 21.7 us  [the longest x8 13.3 us: gather_around(): lax.ppermute(going_up, axis, [(d, (d + 1) % ways) for d in range(ways)])]
    ppermute x1, waiting for transfers between devices: 16.1 us -> 8.56 us  [padded(): before = lax.ppermute(last, axis, up)]
    ppermute x1, starting transfers between devices: 2.17 us -> 8.75 us  [padded(): after = lax.ppermute(first, axis, down)]
    ppermute x1, waiting for transfers between devices: 11.8 us -> 6.51 us  [padded(): after = lax.ppermute(first, axis, down)]
    unnamed x25 -> x27, local copies, waits for them, and re-layouts: 7.56 us -> 7.56 us
  transfers between devices with their start and end apart: 3 -> 17, of which waited for: 3 -> 10; matrix products, arithmetic and copies ran while one was open for 3% -> 4% of each run, Pallas kernels for 0% -> 0%
where the time goes in v1:
time: 213 us; the launch traced here: 212 us
  matrix products  57.4 us (27%)
  starting transfers between devices  47.4 us (22%)
  local copies, waits for them, and re-layouts  44.3 us (21%)
  waiting for transfers between devices  36.8 us (17%)
  other arithmetic  25.6 us (12%)
    ppermute x7, starting transfers between devices, gather_around(): lax.ppermute(going_down, axis, [(d, (d - 1) % ways) for d in range(ways)])  32.5 us
    dot_general x6, matrix products, attend(): jnp.einsum('tn,nhdk->thdk', select, values_t, preferred_element_type=jnp....  23.8 us
    while x42, local copies, waits for them, and re-layouts  14.4 us
    ppermute x8, waiting for transfers between devices, gather_around(): lax.ppermute(going_up, axis, [(d, (d + 1) % ways) for d in range(ways)])  13.3 us
    dot_general x6, matrix products, attend(): jnp.einsum('thdk,thqk->thdq', slot_values, weights.astype(jnp.bfloat16),...  10.8 us
    dot_general x6, matrix products, attend(): jnp.einsum('thdq,thdk->thqk', queries_t, slot_keys, preferred_element_typ...  10.7 us
    reduce_sum x6, other arithmetic, attend(): total = total * factor + jnp.sum(weights, axis=-1)  10 us
    transpose x1, local copies, waits for them, and re-layouts, body(): values_t = nearby.reshape(near_count, OBS, heads, HD).transpose(0, 2, 3, 1)  9.12 us
  transfers between devices with their start and end apart: 17, of which 10 were waited for; matrix products, arithmetic and copies ran while one was open for 4% of the time, Pallas kernels for 0%

profile of v1, /device:TPU:1, one launch (start us, length us, event | category | flops | bytes accessed | tf_op | source)
XLA Modules:
  0.0 212.4 jit_solution(10289929910125441494)
XLA Ops:
  0.0 2.6 %collective-permute-start = (bf16[64,1536]{1,0:T(8,128)(2,1)}, bf16[64,1536]{1,0:T(8,128)(2,1)S(1)}, u32[]{:S(2)}, u32[]{:S(2)}) collective-permute-start(bf16[64,1536]{1,0:T(8,128)(2,1)} %param.19), channel_id=1, source_target_pairs={{0,1},{1,2},{2,3},{3,4},{4,5},{5,6},{6,7},{7,8},{8,9},{9,10},{10,1... | collective-permute-start | bytes 589832 | tf_op jit(solution)/shard_map/ppermute | solution.py:24
  3.5 1.1 mul.160
  6.2 2.8 %collective-permute-start.3 = (bf16[64,1536]{1,0:T(8,128)(2,1)S(1)}, bf16[64,1536]{1,0:T(8,128)(2,1)S(1)}, u32[]{:S(2)}, u32[]{:S(2)}) collective-permute-start(bf16[64,1536]{1,0:T(8,128)(2,1)S(1)} %collective-permute-done.1), channel_id=1, source_target_pairs={{0,15},{1,0},{2,1},{3,2},{4,3},{5,4},{6,5},{7,6},{8,7},{9,8},{10,9... | collective-permute-start | bytes 589832 | tf_op jit(solution)/shard_map/ppermute | solution.py:27
  9.0 1.1 collective-permute-start.2
  10.1 3.2 %collective-permute-done.3 = bf16[64,1536]{1,0:T(8,128)(2,1)S(1)} collective-permute-done((bf16[64,1536]{1,0:T(8,128)(2,1)S(1)}, bf16[64,1536]{1,0:T(8,128)(2,1)S(1)}, u32[]{:S(2)}, u32[]{:S(2)}) %collective-permute-start.3) | collective-permute-done | bytes 196640 | tf_op jit(solution)/shard_map/ppermute | solution.py:27
  13.4 3.3 %collective-permute-start.5 = (bf16[64,1536]{1,0:T(8,128)(2,1)S(1)}, bf16[64,1536]{1,0:T(8,128)(2,1)S(1)}, u32[]{:S(2)}, u32[]{:S(2)}) collective-permute-start(bf16[64,1536]{1,0:T(8,128)(2,1)S(1)} %collective-permute-done.3), channel_id=1, source_target_pairs={{0,15},{1,0},{2,1},{3,2},{4,3},{5,4},{6,5},{7,6},{8,7},{9,8},{10,9... | collective-permute-start | bytes 589832 | tf_op jit(solution)/shard_map/ppermute | solution.py:27
  17.1 1.4 collective-permute-done.5
  18.5 6.0 %collective-permute-start.7 = (bf16[64,1536]{1,0:T(8,128)(2,1)S(1)}, bf16[64,1536]{1,0:T(8,128)(2,1)S(1)}, u32[]{:S(2)}, u32[]{:S(2)}) collective-permute-start(bf16[64,1536]{1,0:T(8,128)(2,1)S(1)} %collective-permute-done.5), channel_id=1, source_target_pairs={{0,15},{1,0},{2,1},{3,2},{4,3},{5,4},{6,5},{7,6},{8,7},{9,8},{10,9... | collective-permute-start | bytes 589832 | tf_op jit(solution)/shard_map/ppermute | solution.py:27
  25.5 6.7 %collective-permute-start.9 = (bf16[64,1536]{1,0:T(8,128)(2,1)S(1)}, bf16[64,1536]{1,0:T(8,128)(2,1)S(1)}, u32[]{:S(2)}, u32[]{:S(2)}) collective-permute-start(bf16[64,1536]{1,0:T(8,128)(2,1)S(1)} %collective-permute-done.7), channel_id=1, source_target_pairs={{0,15},{1,0},{2,1},{3,2},{4,3},{5,4},{6,5},{7,6},{8,7},{9,8},{10,9... | collective-permute-start | bytes 589832 | tf_op jit(solution)/shard_map/ppermute | solution.py:27
  33.3 6.8 %collective-permute-start.11 = (bf16[64,1536]{1,0:T(8,128)(2,1)S(1)}, bf16[64,1536]{1,0:T(8,128)(2,1)S(1)}, u32[]{:S(2)}, u32[]{:S(2)}) collective-permute-start(bf16[64,1536]{1,0:T(8,128)(2,1)S(1)} %collective-permute-done.9), channel_id=1, source_target_pairs={{0,15},{1,0},{2,1},{3,2},{4,3},{5,4},{6,5},{7,6},{8,7},{9,8},{10,9... | collective-permute-start | bytes 589832 | tf_op jit(solution)/shard_map/ppermute | solution.py:27
  41.2 6.8 %collective-permute-start.13 = (bf16[64,1536]{1,0:T(8,128)(2,1)S(1)}, bf16[64,1536]{1,0:T(8,128)(2,1)S(1)}, u32[]{:S(2)}, u32[]{:S(2)}) collective-permute-start(bf16[64,1536]{1,0:T(8,128)(2,1)S(1)} %collective-permute-done.11), channel_id=1, source_target_pairs={{0,15},{1,0},{2,1},{3,2},{4,3},{5,4},{6,5},{7,6},{8,7},{9,8},{10,9... | collective-permute-start | bytes 589832 | tf_op jit(solution)/shard_map/ppermute | solution.py:27
  48.1 5.6 %collective-permute-done.12 = bf16[64,1536]{1,0:T(8,128)(2,1)S(1)} collective-permute-done((bf16[64,1536]{1,0:T(8,128)(2,1)S(1)}, bf16[64,1536]{1,0:T(8,128)(2,1)S(1)}, u32[]{:S(2)}, u32[]{:S(2)}) %collective-permute-start.12) | collective-permute-done | bytes 196640 | tf_op jit(solution)/shard_map/ppermute | solution.py:24
  53.7 7.7 %collective-permute-done.14 = bf16[64,1536]{1,0:T(8,128)(2,1)S(1)} collective-permute-done((bf16[64,1536]{1,0:T(8,128)(2,1)S(1)}, bf16[64,1536]{1,0:T(8,128)(2,1)S(1)}, u32[]{:S(2)}, u32[]{:S(2)}) %collective-permute-start.14) | collective-permute-done | bytes 196640 | tf_op jit(solution)/shard_map/ppermute | solution.py:24
  61.5 3.0 %fusion.30 = bf16[4,128,1536]{2,1,0:T(8,128)(2,1)} fusion(bf16[1024,1536]{1,0:T(8,128)(2,1)S(1)} %constant_dynamic-update-slice_fusion, bf16[4,128,1024]{2,1,0:T(8,128)(2,1)S(1)} %mul.161, bf16[4,1024]{1,0:T(4,128)(2,1)S(1)} %bitcast.76), kind=kOutput, calls=%fused_computation.47 | convolution fusion | flops 1611923456 | bytes 5775360 | tf_op jit(solution)/shard_map/bop,pd->bod/dot_general | solution.py:78
  64.5 8.8 %collective-permute-start.16 = (bf16[4,128,1536]{2,1,0:T(8,128)(2,1)}, bf16[4,128,1536]{2,1,0:T(8,128)(2,1)}, u32[]{:S(2)}, u32[]{:S(2)}) collective-permute-start(bf16[4,128,1536]{2,1,0:T(8,128)(2,1)} %fusion.30), channel_id=1, source_target_pairs={{1,0},{2,1},{3,2},{4,3},{5,4},{6,5},{7,6},{8,7},{9,8},{10,9},{11,1... | collective-permute-start | bytes 4718600 | tf_op jit(solution)/shard_map/ppermute | solution.py:42
  73.2 2.1 collective-permute-start.15
  78.1 1.9 copy.33
  80.0 6.5 %collective-permute-done.16 = bf16[4,128,1536]{2,1,0:T(8,128)(2,1)} collective-permute-done((bf16[4,128,1536]{2,1,0:T(8,128)(2,1)}, bf16[4,128,1536]{2,1,0:T(8,128)(2,1)}, u32[]{:S(2)}, u32[]{:S(2)}) %collective-permute-start.16) | collective-permute-done | bytes 1572896 | tf_op jit(solution)/shard_map/ppermute | solution.py:42
  86.5 8.6 %collective-permute-done.15 = bf16[4,128,1536]{2,1,0:T(8,128)(2,1)} collective-permute-done((bf16[4,128,1536]{2,1,0:T(8,128)(2,1)}, bf16[4,128,1536]{2,1,0:T(8,128)(2,1)}, u32[]{:S(2)}, u32[]{:S(2)}) %collective-permute-start.15) | collective-permute-done | bytes 1572896 | tf_op jit(solution)/shard_map/ppermute | solution.py:41
  95.1 5.7 %multiply_reduce_fusion = (f32[12,128]{1,0:T(8,128)S(1)}, bf16[12,128,1536]{2,1,0:T(8,128)(2,1)}) fusion(bf16[4,128,1536]{2,1,0:T(8,128)(2,1)} %collective-permute-done.16, bf16[4,128,1536]{2,1,0:T(8,128)(2,1)} %fusion.30, bf16[4,128,1536]{2,1,0:T(8,128)(2,1)} %collective-permute-done.15), kind=kLoop, calls=%fused_computation.36 | loop fusion | flops 11794944 | bytes 9443328 | tf_op jit(solution)/shard_map/reduce_sum | solution.py:49
  100.8 2.6 %copy.34 = bf16[4,128,1536]{1,2,0:T(8,128)(2,1)} copy(bf16[4,128,1536]{2,1,0:T(8,128)(2,1)} %collective-permute-done.16) | data formatting | bytes 3145728 | tf_op jit(solution)/shard_map/ppermute | solution.py:42
  103.3 2.6 %copy.32 = bf16[4,128,1536]{1,2,0:T(8,128)(2,1)} copy(bf16[4,128,1536]{2,1,0:T(8,128)(2,1)} %collective-permute-done.15) | data formatting | bytes 3145728 | tf_op jit(solution)/shard_map/ppermute | solution.py:41
  105.9 3.7 %fusion.26 = bf16[12,24,64,128]{3,2,1,0:T(8,128)(2,1)S(1)} fusion(bf16[4,128,24,64]{1,3,2,0:T(8,128)(2,1)} %bitcast.73, bf16[4,128,24,64]{1,3,2,0:T(8,128)(2,1)S(1)} %bitcast.72, bf16[4,128,24,64]{1,3,2,0:T(8,128)(2,1)} %bitcast.74, f32[24,64]{1,0:T(8,128)S(1)} %mul.186, f32[12,128]{1,0:T(8,128)S(1)} %add_rsqrt_fusion), kind=kLoop, calls=%fused_computation.37 | loop fusion | flops 14155776 | bytes 9449472 | tf_op jit(solution)/shard_map/transpose | solution.py:86
  109.6 6.9 %copy.37 = bf16[12,24,64,128]{3,0,2,1:T(8,128)(2,1)} copy(bf16[12,24,64,128]{3,2,1,0:T(8,128)(2,1)S(1)} %fusion.26) | data formatting | bytes 9437184
  116.5 9.1 %copy.43 = bf16[12,128,1536]{1,0,2:T(8,128)(2,1)} copy(bf16[12,128,1536]{2,1,0:T(8,128)(2,1)} %get-tuple-element.287) | data formatting | bytes 9437184 | tf_op jit(solution)/shard_map/transpose | solution.py:87
  125.6 78.2 %while.18 = (s32[]{:T(128)}, f32[4,24,128]{2,1,0:T(8,128)S(1)}, f32[4,24,128]{2,1,0:T(8,128)S(1)}, f32[4,24,64,128]{3,2,1,0:T(8,128)}, s32[4]{0:T(128)S(1)}, /*i...) while((s32[]{:T(128)}, f32[4,24,128]{2,1,0:T(8,128)S(1)}, ...), condition=%wide.region_5.6_spmd.clone, body=%wide.region_1.5_spmd.clone.sunk | while | flops 461698304 | bytes 87296416 | solution.py:131
  125.9 4.0 %convolution_convert_fusion.5 = bf16[4,24,64,128]{3,0,2,1:T(4,128)(2,1)S(1)} fusion(bf16[12,24,64,128]{3,0,2,1:T(8,128)(2,1)} %get-tuple-element.394, s32[4]{0:T(128)S(1)} %dynamic-slice_bitcast_fusion.2), kind=kOutput, calls=%fused_computation.14.clone.1 | convolution fusion | flops 19660848 | bytes 6291472 | tf_op jit(solution)/shard_map/while/body/eval_jaxpr/tn,nhdk->thdk/dot_general | solution.py:103
  130.5 1.0 convolution_convert_fusion.4
  131.6 1.8 select_reduce_fusion.2
  133.4 1.7 bitcast_reduce_fusion.2
  135.3 1.8 fusion.63
  137.1 1.6 copy-done.4
  139.0 4.0 %convolution_convert_fusion.5 = bf16[4,24,64,128]{3,0,2,1:T(4,128)(2,1)S(1)} fusion(bf16[12,24,64,128]{3,0,2,1:T(8,128)(2,1)} %get-tuple-element.394, s32[4]{0:T(128)S(1)} %dynamic-slice_bitcast_fusion.2), kind=kOutput, calls=%fused_computation.14.clone.1 | convolution fusion | flops 19660848 | bytes 6291472 | tf_op jit(solution)/shard_map/while/body/eval_jaxpr/tn,nhdk->thdk/dot_general | solution.py:103
  143.6 1.0 convolution_convert_fusion.4
  144.6 1.8 select_reduce_fusion.2
  146.4 1.7 bitcast_reduce_fusion.2
  148.3 1.8 fusion.63
  150.1 1.6 copy-done.4
  152.0 4.0 %convolution_convert_fusion.5 = bf16[4,24,64,128]{3,0,2,1:T(4,128)(2,1)S(1)} fusion(bf16[12,24,64,128]{3,0,2,1:T(8,128)(2,1)} %get-tuple-element.394, s32[4]{0:T(128)S(1)} %dynamic-slice_bitcast_fusion.2), kind=kOutput, calls=%fused_computation.14.clone.1 | convolution fusion | flops 19660848 | bytes 6291472 | tf_op jit(solution)/shard_map/while/body/eval_jaxpr/tn,nhdk->thdk/dot_general | solution.py:103
  156.6 1.0 convolution_convert_fusion.4
  157.6 1.8 select_reduce_fusion.2
  159.5 1.7 bitcast_reduce_fusion.2
  161.3 1.8 fusion.63
  163.2 1.6 copy-done.4
  165.0 4.0 %convolution_convert_fusion.5 = bf16[4,24,64,128]{3,0,2,1:T(4,128)(2,1)S(1)} fusion(bf16[12,24,64,128]{3,0,2,1:T(8,128)(2,1)} %get-tuple-element.394, s32[4]{0:T(128)S(1)} %dynamic-slice_bitcast_fusion.2), kind=kOutput, calls=%fused_computation.14.clone.1 | convolution fusion | flops 19660848 | bytes 6291472 | tf_op jit(solution)/shard_map/while/body/eval_jaxpr/tn,nhdk->thdk/dot_general | solution.py:103
  169.6 1.0 convolution_convert_fusion.4
  170.7 1.8 select_reduce_fusion.2
  172.5 1.7 bitcast_reduce_fusion.2
  174.4 1.8 fusion.63
  176.2 1.6 copy-done.4
  178.1 4.0 %convolution_convert_fusion.5 = bf16[4,24,64,128]{3,0,2,1:T(4,128)(2,1)S(1)} fusion(bf16[12,24,64,128]{3,0,2,1:T(8,128)(2,1)} %get-tuple-element.394, s32[4]{0:T(128)S(1)} %dynamic-slice_bitcast_fusion.2), kind=kOutput, calls=%fused_computation.14.clone.1 | convolution fusion | flops 19660848 | bytes 6291472 | tf_op jit(solution)/shard_map/while/body/eval_jaxpr/tn,nhdk->thdk/dot_general | solution.py:103
  183.7 1.8 select_reduce_fusion.2
  185.5 1.7 bitcast_reduce_fusion.2
  187.4 1.8 fusion.63
  189.2 1.6 copy-done.4
  191.1 4.0 %convolution_convert_fusion.5 = bf16[4,24,64,128]{3,0,2,1:T(4,128)(2,1)S(1)} fusion(bf16[12,24,64,128]{3,0,2,1:T(8,128)(2,1)} %get-tuple-element.394, s32[4]{0:T(128)S(1)} %dynamic-slice_bitcast_fusion.2), kind=kOutput, calls=%fused_computation.14.clone.1 | convolution fusion | flops 19660848 | bytes 6291472 | tf_op jit(solution)/shard_map/while/body/eval_jaxpr/tn,nhdk->thdk/dot_general | solution.py:103
  196.7 1.8 select_reduce_fusion.2
  198.6 1.7 bitcast_reduce_fusion.2
  200.4 1.8 fusion.63
  202.3 1.6 copy-done.4
  203.9 2.5 %fusion.35 = bf16[4,128,24,64]{1,3,2,0:T(8,128)(2,1)S(1)} fusion(f32[4,24,64,128]{3,2,1,0:T(8,128)} %get-tuple-element.205, f32[4,24,128]{2,1,0:T(8,128)S(1)} %get-tuple-element.206), kind=kLoop, calls=%fused_computation.50 | loop fusion | flops 1572864 | bytes 4767744 | tf_op jit(solution)/shard_map/transpose | solution.py:135
  206.4 1.4 copy.40
  207.9 3.0 %multiply_reduce_fusion.1 = (f32[512]{0:T(512)S(1)}, f32[512,1536]{1,0:T(8,128)S(1)}) fusion(bf16[1536,1536]{1,0:T(8,128)(2,1)S(1)} %copy-done.12, bf16[192,8,4,128]{3,2,1,0:T(4,128)(2,1)S(1)} %bitcast.75, bf16[512,1536]{1,0:T(8,128)(2,1)S(1)} %copy-done.6), kind=kOutput, calls=%fused_computation.45 | convolution fusion | flops 2419064320 | bytes 11012096 | tf_op jit(solution)/shard_map/dot_general | solution.py:138
  210.9 1.5 multiply_convert_fusion.1
  (151 shorter events, 17.5 us)
Async XLA Ops:
  0.0 77.4 %copy-start = (s32[64]{0:T(128)S(1)}, s32[64]{0:T(128)}, u32[]{:S(2)}) copy-start(s32[64]{0:T(128)} %param.21) | copy-start | bytes 772
  0.0 6.2 %collective-permute-start.1 = (bf16[64,1536]{1,0:T(8,128)(2,1)}, bf16[64,1536]{1,0:T(8,128)(2,1)S(1)}, u32[]{:S(2)}, u32[]{:S(2)}) collective-permute-start(bf16[64,1536]{1,0:T(8,128)(2,1)} %param.19), channel_id=1, source_target_pairs={{0,15},{1,0},{2,1},{3,2},{4,3},{5,4},{6,5},{7,6},{8,7},{9,8},{10,9... | collective-permute-start | bytes 589832 | tf_op jit(solution)/shard_map/ppermute | solution.py:27
  0.0 9.0 %collective-permute-start = (bf16[64,1536]{1,0:T(8,128)(2,1)}, bf16[64,1536]{1,0:T(8,128)(2,1)S(1)}, u32[]{:S(2)}, u32[]{:S(2)}) collective-permute-start(bf16[64,1536]{1,0:T(8,128)(2,1)} %param.19), channel_id=1, source_target_pairs={{0,1},{1,2},{2,3},{3,4},{4,5},{5,6},{6,7},{7,8},{8,9},{9,10},{10,1... | collective-permute-start | bytes 589832 | tf_op jit(solution)/shard_map/ppermute | solution.py:24
  3.5 1.9 copy-start.7
  6.2 7.2 %collective-permute-start.3 = (bf16[64,1536]{1,0:T(8,128)(2,1)S(1)}, bf16[64,1536]{1,0:T(8,128)(2,1)S(1)}, u32[]{:S(2)}, u32[]{:S(2)}) collective-permute-start(bf16[64,1536]{1,0:T(8,128)(2,1)S(1)} %collective-permute-done.1), channel_id=1, source_target_pairs={{0,15},{1,0},{2,1},{3,2},{4,3},{5,4},{6,5},{7,6},{8,7},{9,8},{10,9... | collective-permute-start | bytes 589832 | tf_op jit(solution)/shard_map/ppermute | solution.py:27
  9.0 7.7 %collective-permute-start.2 = (bf16[64,1536]{1,0:T(8,128)(2,1)S(1)}, bf16[64,1536]{1,0:T(8,128)(2,1)S(1)}, u32[]{:S(2)}, u32[]{:S(2)}) collective-permute-start(bf16[64,1536]{1,0:T(8,128)(2,1)S(1)} %collective-permute-done), channel_id=1, source_target_pairs={{0,1},{1,2},{2,3},{3,4},{4,5},{5,6},{6,7},{7,8},{8,9},{9,10},{10,1... | collective-permute-start | bytes 589832 | tf_op jit(solution)/shard_map/ppermute | solution.py:24
  13.4 5.1 %collective-permute-start.5 = (bf16[64,1536]{1,0:T(8,128)(2,1)S(1)}, bf16[64,1536]{1,0:T(8,128)(2,1)S(1)}, u32[]{:S(2)}, u32[]{:S(2)}) collective-permute-start(bf16[64,1536]{1,0:T(8,128)(2,1)S(1)} %collective-permute-done.3), channel_id=1, source_target_pairs={{0,15},{1,0},{2,1},{3,2},{4,3},{5,4},{6,5},{7,6},{8,7},{9,8},{10,9... | collective-permute-start | bytes 589832 | tf_op jit(solution)/shard_map/ppermute | solution.py:27
  16.7 7.8 %collective-permute-start.4 = (bf16[64,1536]{1,0:T(8,128)(2,1)S(1)}, bf16[64,1536]{1,0:T(8,128)(2,1)S(1)}, u32[]{:S(2)}, u32[]{:S(2)}) collective-permute-start(bf16[64,1536]{1,0:T(8,128)(2,1)S(1)} %collective-permute-done.2), channel_id=1, source_target_pairs={{0,1},{1,2},{2,3},{3,4},{4,5},{5,6},{6,7},{7,8},{8,9},{9,10},{10,1... | collective-permute-start | bytes 589832 | tf_op jit(solution)/shard_map/ppermute | solution.py:24
  18.5 7.1 %collective-permute-start.7 = (bf16[64,1536]{1,0:T(8,128)(2,1)S(1)}, bf16[64,1536]{1,0:T(8,128)(2,1)S(1)}, u32[]{:S(2)}, u32[]{:S(2)}) collective-permute-start(bf16[64,1536]{1,0:T(8,128)(2,1)S(1)} %collective-permute-done.5), channel_id=1, source_target_pairs={{0,15},{1,0},{2,1},{3,2},{4,3},{5,4},{6,5},{7,6},{8,7},{9,8},{10,9... | collective-permute-start | bytes 589832 | tf_op jit(solution)/shard_map/ppermute | solution.py:27
  24.5 7.8 %collective-permute-start.6 = (bf16[64,1536]{1,0:T(8,128)(2,1)S(1)}, bf16[64,1536]{1,0:T(8,128)(2,1)S(1)}, u32[]{:S(2)}, u32[]{:S(2)}) collective-permute-start(bf16[64,1536]{1,0:T(8,128)(2,1)S(1)} %collective-permute-done.4), channel_id=1, source_target_pairs={{0,1},{1,2},{2,3},{3,4},{4,5},{5,6},{6,7},{7,8},{8,9},{9,10},{10,1... | collective-permute-start | bytes 589832 | tf_op jit(solution)/shard_map/ppermute | solution.py:24
  25.5 7.8 %collective-permute-start.9 = (bf16[64,1536]{1,0:T(8,128)(2,1)S(1)}, bf16[64,1536]{1,0:T(8,128)(2,1)S(1)}, u32[]{:S(2)}, u32[]{:S(2)}) collective-permute-start(bf16[64,1536]{1,0:T(8,128)(2,1)S(1)} %collective-permute-done.7), channel_id=1, source_target_pairs={{0,15},{1,0},{2,1},{3,2},{4,3},{5,4},{6,5},{7,6},{8,7},{9,8},{10,9... | collective-permute-start | bytes 589832 | tf_op jit(solution)/shard_map/ppermute | solution.py:27
  32.2 7.9 %collective-permute-start.8 = (bf16[64,1536]{1,0:T(8,128)(2,1)S(1)}, bf16[64,1536]{1,0:T(8,128)(2,1)S(1)}, u32[]{:S(2)}, u32[]{:S(2)}) collective-permute-start(bf16[64,1536]{1,0:T(8,128)(2,1)S(1)} %collective-permute-done.6), channel_id=1, source_target_pairs={{0,1},{1,2},{2,3},{3,4},{4,5},{5,6},{6,7},{7,8},{8,9},{9,10},{10,1... | collective-permute-start | bytes 589832 | tf_op jit(solution)/shard_map/ppermute | solution.py:24
  33.3 7.9 %collective-permute-start.11 = (bf16[64,1536]{1,0:T(8,128)(2,1)S(1)}, bf16[64,1536]{1,0:T(8,128)(2,1)S(1)}, u32[]{:S(2)}, u32[]{:S(2)}) collective-permute-start(bf16[64,1536]{1,0:T(8,128)(2,1)S(1)} %collective-permute-done.9), channel_id=1, source_target_pairs={{0,15},{1,0},{2,1},{3,2},{4,3},{5,4},{6,5},{7,6},{8,7},{9,8},{10,9... | collective-permute-start | bytes 589832 | tf_op jit(solution)/shard_map/ppermute | solution.py:27
  40.1 7.9 %collective-permute-start.10 = (bf16[64,1536]{1,0:T(8,128)(2,1)S(1)}, bf16[64,1536]{1,0:T(8,128)(2,1)S(1)}, u32[]{:S(2)}, u32[]{:S(2)}) collective-permute-start(bf16[64,1536]{1,0:T(8,128)(2,1)S(1)} %collective-permute-done.8), channel_id=1, source_target_pairs={{0,1},{1,2},{2,3},{3,4},{4,5},{5,6},{6,7},{7,8},{8,9},{9,10},{10,1... | collective-permute-start | bytes 589832 | tf_op jit(solution)/shard_map/ppermute | solution.py:24
  41.2 12.5 %collective-permute-start.13 = (bf16[64,1536]{1,0:T(8,128)(2,1)S(1)}, bf16[64,1536]{1,0:T(8,128)(2,1)S(1)}, u32[]{:S(2)}, u32[]{:S(2)}) collective-permute-start(bf16[64,1536]{1,0:T(8,128)(2,1)S(1)} %collective-permute-done.11), channel_id=1, source_target_pairs={{0,15},{1,0},{2,1},{3,2},{4,3},{5,4},{6,5},{7,6},{8,7},{9,8},{10,9... | collective-permute-start | bytes 589832 | tf_op jit(solution)/shard_map/ppermute | solution.py:27
  48.0 5.6 %collective-permute-start.12 = (bf16[64,1536]{1,0:T(8,128)(2,1)S(1)}, bf16[64,1536]{1,0:T(8,128)(2,1)S(1)}, u32[]{:S(2)}, u32[]{:S(2)}) collective-permute-start(bf16[64,1536]{1,0:T(8,128)(2,1)S(1)} %collective-permute-done.10), channel_id=1, source_target_pairs={{0,1},{1,2},{2,3},{3,4},{4,5},{5,6},{6,7},{7,8},{8,9},{9,10},{10,1... | collective-permute-start | bytes 589832 | tf_op jit(solution)/shard_map/ppermute | solution.py:24
  53.7 7.8 %collective-permute-start.14 = (bf16[64,1536]{1,0:T(8,128)(2,1)S(1)}, bf16[64,1536]{1,0:T(8,128)(2,1)S(1)}, u32[]{:S(2)}, u32[]{:S(2)}) collective-permute-start(bf16[64,1536]{1,0:T(8,128)(2,1)S(1)} %collective-permute-done.12), channel_id=1, source_target_pairs={{0,1},{1,2},{2,3},{3,4},{4,5},{5,6},{6,7},{7,8},{8,9},{9,10},{10,1... | collective-permute-start | bytes 589832 | tf_op jit(solution)/shard_map/ppermute | solution.py:24
  61.5 13.9 %copy-start.11 = (s32[4,6]{1,0:T(4,128)S(1)}, s32[4,6]{1,0:T(4,128)}, u32[]{:S(2)}) copy-start(s32[4,6]{1,0:T(4,128)} %param.22) | copy-start | bytes 292
  61.5 14.0 %copy-start.10 = (f32[1536]{0:T(1024)S(1)}, f32[1536]{0:T(1024)}, u32[]{:S(2)}) copy-start(f32[1536]{0:T(1024)} %param.15) | copy-start | bytes 18436
  61.5 14.1 %copy-start.5 = (bf16[512,1536]{1,0:T(8,128)(2,1)S(1)}, bf16[512,1536]{1,0:T(8,128)(2,1)}, u32[]{:S(2)}) copy-start(bf16[512,1536]{1,0:T(8,128)(2,1)} %param.13) | copy-start | bytes 4718596
  61.5 14.0 %copy-start.8 = (f32[1536]{0:T(1024)S(1)}, f32[1536]{0:T(1024)}, u32[]{:S(2)}) copy-start(f32[1536]{0:T(1024)} %param.14) | copy-start | bytes 18436
  64.5 22.0 %collective-permute-start.16 = (bf16[4,128,1536]{2,1,0:T(8,128)(2,1)}, bf16[4,128,1536]{2,1,0:T(8,128)(2,1)}, u32[]{:S(2)}, u32[]{:S(2)}) collective-permute-start(bf16[4,128,1536]{2,1,0:T(8,128)(2,1)} %fusion.30), channel_id=1, source_target_pairs={{1,0},{2,1},{3,2},{4,3},{5,4},{6,5},{7,6},{8,7},{9,8},{10,9},{11,1... | collective-permute-start | bytes 4718600 | tf_op jit(solution)/shard_map/ppermute | solution.py:42
  73.2 21.8 %collective-permute-start.15 = (bf16[4,128,1536]{2,1,0:T(8,128)(2,1)}, bf16[4,128,1536]{2,1,0:T(8,128)(2,1)}, u32[]{:S(2)}, u32[]{:S(2)}) collective-permute-start(bf16[4,128,1536]{2,1,0:T(8,128)(2,1)} %fusion.30), channel_id=1, source_target_pairs={{0,1},{1,2},{2,3},{3,4},{4,5},{5,6},{6,7},{7,8},{8,9},{9,10},{10,1... | collective-permute-start | bytes 4718600 | tf_op jit(solution)/shard_map/ppermute | solution.py:41
  116.5 9.1 %copy-start.13 = (s32[4]{0:T(128)S(1)}, s32[4]{0:T(128)}, u32[]{:S(2)}) copy-start(s32[4]{0:T(128)} %param.23) | copy-start | bytes 52
  125.9 4.6 %copy-start.2 = (bf16[12,24,64,128]{3,0,2,1:T(8,128)(2,1)S(1)}, bf16[12,24,64,128]{3,0,2,1:T(8,128)(2,1)}, u32[]{:S(2)}) copy-start(bf16[12,24,64,128]{3,0,2,1:T(8,128)(2,1)} %get-tuple-element.392) | copy-start | bytes 14155780 | tf_op jit(solution)/shard_map/while
  133.4 1.9 copy-start.3
  137.1 1.6 copy-start.4
  139.0 4.6 %copy-start.2 = (bf16[12,24,64,128]{3,0,2,1:T(8,128)(2,1)S(1)}, bf16[12,24,64,128]{3,0,2,1:T(8,128)(2,1)}, u32[]{:S(2)}) copy-start(bf16[12,24,64,128]{3,0,2,1:T(8,128)(2,1)} %get-tuple-element.392) | copy-start | bytes 14155780 | tf_op jit(solution)/shard_map/while
  146.4 1.9 copy-start.3
  150.1 1.6 copy-start.4
  152.0 4.6 %copy-start.2 = (bf16[12,24,64,128]{3,0,2,1:T(8,128)(2,1)S(1)}, bf16[12,24,64,128]{3,0,2,1:T(8,128)(2,1)}, u32[]{:S(2)}) copy-start(bf16[12,24,64,128]{3,0,2,1:T(8,128)(2,1)} %get-tuple-element.392) | copy-start | bytes 14155780 | tf_op jit(solution)/shard_map/while
  159.4 1.9 copy-start.3
  163.1 1.6 copy-start.4
  165.0 4.6 %copy-start.2 = (bf16[12,24,64,128]{3,0,2,1:T(8,128)(2,1)S(1)}, bf16[12,24,64,128]{3,0,2,1:T(8,128)(2,1)}, u32[]{:S(2)}) copy-start(bf16[12,24,64,128]{3,0,2,1:T(8,128)(2,1)} %get-tuple-element.392) | copy-start | bytes 14155780 | tf_op jit(solution)/shard_map/while
  172.5 1.9 copy-start.3
  176.2 1.6 copy-start.4
  178.1 4.6 %copy-start.2 = (bf16[12,24,64,128]{3,0,2,1:T(8,128)(2,1)S(1)}, bf16[12,24,64,128]{3,0,2,1:T(8,128)(2,1)}, u32[]{:S(2)}) copy-start(bf16[12,24,64,128]{3,0,2,1:T(8,128)(2,1)} %get-tuple-element.392) | copy-start | bytes 14155780 | tf_op jit(solution)/shard_map/while
  185.5 1.9 copy-start.3
  189.2 1.6 copy-start.4
  191.1 4.6 %copy-start.2 = (bf16[12,24,64,128]{3,0,2,1:T(8,128)(2,1)S(1)}, bf16[12,24,64,128]{3,0,2,1:T(8,128)(2,1)}, u32[]{:S(2)}) copy-start(bf16[12,24,64,128]{3,0,2,1:T(8,128)(2,1)} %get-tuple-element.392) | copy-start | bytes 14155780 | tf_op jit(solution)/shard_map/while
  198.6 1.9 copy-start.3
  202.2 1.6 copy-start.4
  203.9 4.0 %copy-start.6 = (bf16[512,1536]{1,0:T(8,128)(2,1)S(1)}, bf16[512,1536]{1,0:T(8,128)(2,1)}, u32[]{:S(2)}) copy-start(bf16[512,1536]{1,0:T(8,128)(2,1)} %param.13) | copy-start | bytes 4718596
  203.9 4.0 %copy-start.12 = (bf16[1536,1536]{1,0:T(8,128)(2,1)S(1)}, bf16[1536,1536]{1,0:T(8,128)(2,1)}, u32[]{:S(2)}) copy-start(bf16[1536,1536]{1,0:T(8,128)(2,1)} %param.17) | copy-start | bytes 14155780
  207.9 3.0 %copy-start.9 = (f32[1536]{0:T(1024)S(1)}, f32[1536]{0:T(1024)}, u32[]{:S(2)}) copy-start(f32[1536]{0:T(1024)} %param.16) | copy-start | bytes 18436
  207.9 4.5 %copy-start.1 = (s32[64]{0:T(128)S(1)}, s32[64]{0:T(128)}, u32[]{:S(2)}) copy-start(s32[64]{0:T(128)} %param.21) | copy-start | bytes 772
